TPU v7x, 32 devices: a whole 2x2x4 slice. The times are simulated.
32 devices in a mesh: fsdp: 8 (over z, y), rows: 4 (over x, core).
Axes of the slice: x: 2, y: 2, z: 4, core: 2. Of those that a mesh axis runs over, the one named last changes fastest.
Arguments:
- frames: bfloat16 [8, 12, 16, 1536], P('fsdp', 'rows'), may hold values from -6 to 6
- kernel: float32 [7, 7, 1536], replicated, may hold values from -0.875 to 0.875
- kernel_bias: float32 [1536], replicated, may hold values from -3 to 3
- layer_norm_weight: float32 [1536], replicated, may hold values from 0.25 to 1.75
- layer_norm_bias: float32 [1536], replicated, may hold values from -3 to 3
- up_weight: bfloat16 [1536, 6144], P('fsdp', 'rows'), may hold values from -1 to 1, as said below
- up_bias: float32 [6144], P('rows'), may hold values from -3 to 3
- grn_gamma: float32 [6144], P('rows'), may hold values from 0.2 to 1
- grn_beta: float32 [6144], P('rows'), may hold values from -3 to 3
- grad_out: bfloat16 [8, 12, 16, 6144], P('fsdp', None, None, 'rows'), may hold values from -8 to 8, as said below
Outputs:
- activation: bfloat16 [8, 12, 16, 6144], P('fsdp', None, None, 'rows')
- frames_grad: bfloat16 [8, 12, 16, 1536], P('fsdp', 'rows')
- up_weight_grad: float32 [1536, 6144], P('fsdp', 'rows')
- kernel_grad: float32 [7, 7, 1536], replicated
Inputs may be any that keep to these rules, and one draw needn't show every extreme that they name: `up_weight`: entries lie within the bounds. `grad_out`: entries lie within the bounds.
All inputs are finite; a program needn't handle non-finite values.
Results may differ from a plain program's by a relative error of at most 0.014.
Values may be sent and summed in bfloat16 or wider, within the bound.
No kernel may reach another device: no remote copies, remote signals or barrier semaphores. Data moves between devices by JAX's collectives and lax.ppermute only.
A program may use at most 64 MiB of HBM per device.

v0:
```python
import functools
import jax
import jax.numpy as jnp
from jax import lax
from jax.sharding import PartitionSpec as P

FF = 6144


def extended(block, sides, width):
    for axis, dim in sides:
        count = lax.axis_size(axis)
        forward = [(i, i + 1) for i in range(count - 1)]
        backward = [(target, source) for source, target in forward]
        low = lax.ppermute(
            lax.slice_in_dim(block, block.shape[dim] - width, None, axis=dim), axis, forward
        )
        high = lax.ppermute(lax.slice_in_dim(block, 0, width, axis=dim), axis, backward)
        block = jnp.concatenate([low, block, high], axis=dim)
    return block


def _bit_steps(axes):
    steps = []
    for axis in axes:
        size = lax.axis_size(axis)
        assert size & size - 1 == 0
        mask = 1
        while mask < size:
            steps.append((axis, mask, size))
            mask *= 2
    return steps


def tree_allreduce(value, axes):
    shape = value.shape
    flat = value.reshape(-1)
    steps = _bit_steps(axes)
    assert flat.shape[0] % (1 << len(steps)) == 0
    bits = []
    for axis, mask, size in steps:
        bit = lax.axis_index(axis) // mask % 2
        bits.append(bit)
        halves = flat.reshape(2, -1)
        keep = lax.dynamic_index_in_dim(halves, bit, keepdims=False)
        give = lax.dynamic_index_in_dim(halves, 1 - bit, keepdims=False)
        perm = [(j, j ^ mask) for j in range(size)]
        flat = keep + lax.ppermute(give, axis, perm)
    for (axis, mask, size), bit in reversed(list(zip(steps, bits))):
        perm = [(j, j ^ mask) for j in range(size)]
        other = lax.ppermute(flat, axis, perm)
        flat = jnp.where(bit == 0, jnp.concatenate([flat, other]), jnp.concatenate([other, flat]))
    return flat.reshape(shape)


def tree_reduce_scatter(chunks, axis):
    size = lax.axis_size(axis)
    assert chunks.shape[0] == size and size & size - 1 == 0
    me = lax.axis_index(axis)
    data = chunks
    mask = 1
    while mask < size:
        bit = me // mask % 2
        pairs = data.reshape((data.shape[0] // 2, 2) + data.shape[1:])
        keep = lax.dynamic_index_in_dim(pairs, bit, axis=1, keepdims=False)
        give = lax.dynamic_index_in_dim(pairs, 1 - bit, axis=1, keepdims=False)
        perm = [(j, j ^ mask) for j in range(size)]
        data = keep.astype(jnp.float32) + lax.ppermute(give, axis, perm).astype(jnp.float32)
        mask *= 2
    return data[0]


def fsdp_ring(mesh):
    count = mesh.shape["fsdp"]
    try:
        members = [mesh.devices[j, 0] for j in range(count)]
        spots = [(d.coords[2], d.coords[1]) for d in members]
        zs = sorted({z for z, _ in spots})
        ys = sorted({y for _, y in spots})
        rows_a, cols_b = (len(zs), len(ys))
        where = {(zs.index(z), ys.index(y)): j for j, (z, y) in enumerate(spots)}
        assert len(where) == count == rows_a * cols_b and rows_a % 2 == 0 and (cols_b >= 2)
        cells = [(a, 0) for a in range(rows_a)]
        for k, a in enumerate(range(rows_a - 1, -1, -1)):
            span = range(1, cols_b) if k % 2 == 0 else range(cols_b - 1, 0, -1)
            cells += [(a, b) for b in span]
        ring = [where[c] for c in cells]
        assert sorted(ring) == list(range(count))
    except Exception:
        ring = list(range(count))
    return ring


def ring_all_gather(block, axis, ring, held=None):
    count = len(ring)
    place = [0] * count
    for k, j in enumerate(ring):
        place[j] = k
    ring_arr = jnp.array(ring, jnp.int32)
    me = lax.axis_index(axis)
    spot = jnp.array(place, jnp.int32)[me]
    forward = [(ring[k], ring[(k + 1) % count]) for k in range(count)]
    backward = [(ring[k], ring[(k - 1) % count]) for k in range(count)]
    ahead = count // 2
    behind = count - 1 - ahead
    gathered = jnp.zeros((count,) + block.shape, block.dtype)
    gathered = lax.dynamic_update_index_in_dim(gathered, block, me, 0)
    cw = block
    ccw = block
    for s in range(1, ahead + 1):
        cw = lax.ppermute(cw, axis, forward)
        if s <= behind:
            ccw = lax.ppermute(ccw, axis, backward)
        if s == 1 and held is not None:
            cw, ccw, held = lax.optimization_barrier((cw, ccw, held))
        gathered = lax.dynamic_update_index_in_dim(gathered, cw, ring_arr[(spot - s) % count], 0)
        if s <= behind:
            gathered = lax.dynamic_update_index_in_dim(
                gathered, ccw, ring_arr[(spot + s) % count], 0
            )
    return (gathered.reshape((count * block.shape[0],) + block.shape[1:]), held)


def ring_reduce_scatter(terms, axis, ring):
    count = len(ring)
    place = [0] * count
    for k, j in enumerate(ring):
        place[j] = k
    ring_arr = jnp.array(ring, jnp.int32)
    me = lax.axis_index(axis)
    spot = jnp.array(place, jnp.int32)[me]
    forward = [(ring[k], ring[(k + 1) % count]) for k in range(count)]
    backward = [(ring[k], ring[(k - 1) % count]) for k in range(count)]
    ahead = count // 2
    behind = count - 1 - ahead

    def term(offset):
        return lax.dynamic_index_in_dim(terms, ring_arr[(spot + offset) % count], 0, keepdims=False)

    total = term(0).astype(jnp.float32)
    cw = term(ahead)
    ccw = term(-behind) if behind else None
    for s in range(1, ahead + 1):
        cw = lax.ppermute(cw, axis, forward)
        if s <= behind:
            ccw = lax.ppermute(ccw, axis, backward)
        if s < ahead:
            cw = (cw.astype(jnp.float32) + term(ahead - s).astype(jnp.float32)).astype(terms.dtype)
        else:
            total = total + cw.astype(jnp.float32)
        if s < behind:
            ccw = (ccw.astype(jnp.float32) + term(s - behind).astype(jnp.float32)).astype(
                terms.dtype
            )
        elif s == behind:
            total = total + ccw.astype(jnp.float32)
    return total


def tree_all_gather(block, axis):
    size = lax.axis_size(axis)
    assert size & size - 1 == 0
    me = lax.axis_index(axis)
    data = block[None]
    mask = 1
    while mask < size:
        bit = me // mask % 2
        perm = [(j, j ^ mask) for j in range(size)]
        other = lax.ppermute(data, axis, perm)
        data = jnp.where(bit == 0, jnp.concatenate([data, other]), jnp.concatenate([other, data]))
        mask *= 2
    return data.reshape((size * block.shape[0],) + block.shape[1:])


def conv_rows(framed, kern, kbias):
    rows = framed.shape[0] - 6
    cols = framed.shape[1]
    wide = jnp.pad(framed, ((0, 0), (3, 3), (0, 0)))
    total = jnp.zeros((rows, cols, framed.shape[2]), jnp.float32) + kbias
    for i in range(kern.shape[0]):
        for j in range(kern.shape[1]):
            total = total + wide[i : i + rows, j : j + cols].astype(jnp.float32) * kern[i, j]
    return total


def back_conv(grad_pad, kern):
    rows = grad_pad.shape[0] - 6
    cols = grad_pad.shape[1]
    wide = jnp.pad(grad_pad, ((0, 0), (3, 3), (0, 0)))
    total = jnp.zeros((rows, cols, grad_pad.shape[2]), jnp.float32)
    for i in range(kern.shape[0]):
        for j in range(kern.shape[1]):
            total = (
                total
                + wide[6 - i : 6 - i + rows, 6 - j : 6 - j + cols].astype(jnp.float32) * kern[i, j]
            )
    return total


def kern_grad(framed, grad_rows):
    rows = grad_rows.shape[0]
    cols = grad_rows.shape[1]
    wide = jnp.pad(framed, ((0, 0), (3, 3), (0, 0)))
    grad_f = grad_rows.astype(jnp.float32)
    parts = []
    for i in range(7):
        for j in range(7):
            parts.append(
                jnp.sum(wide[i : i + rows, j : j + cols].astype(jnp.float32) * grad_f, axis=(0, 1))
            )
    return jnp.stack(parts).reshape(7, 7, grad_rows.shape[2])


def apply_layer_norm(activation_rows, scale_factor, offset_bias):
    centered_input = activation_rows - jnp.mean(activation_rows, axis=-1, keepdims=True)
    inverse_deviation = lax.rsqrt(
        jnp.mean(centered_input * centered_input, axis=-1, keepdims=True) + 1e-06
    )
    standardized_input = centered_input * inverse_deviation
    return (
        (standardized_input * scale_factor + offset_bias).astype(jnp.bfloat16),
        standardized_input,
        inverse_deviation,
    )


def gelu_grad(value):
    return (
        0.5 * (1.0 + jax.scipy.special.erf(value * 0.7071067811865476))
        + value * jnp.exp(-0.5 * value * value) * 0.3989422804014327
    )


def layer_norm_backward(normed_input_gradient, scale_factor, standardized_input, inverse_deviation):
    scaled_output = normed_input_gradient * scale_factor
    return (
        inverse_deviation
        * (
            scaled_output
            - jnp.mean(scaled_output, axis=-1, keepdims=True)
            - standardized_input
            * jnp.mean(scaled_output * standardized_input, axis=-1, keepdims=True)
        )
    ).astype(jnp.bfloat16)


def body(
    ring,
    frames,
    kernel,
    kernel_bias,
    layer_norm_weight,
    layer_norm_bias,
    up_weight,
    up_bias,
    grn_gamma,
    grn_beta,
    grad_out,
):
    slab = frames[0]
    chans = slab.shape[2]
    columns, slab = ring_all_gather(up_weight, "fsdp", ring, slab)
    padded = extended(slab, (("rows", 0),), 3)
    activation_rows = conv_rows(padded, kernel, kernel_bias)
    normed_output, standardized_input, inverse_deviation = apply_layer_norm(
        activation_rows, layer_norm_weight, layer_norm_bias
    )
    whole = tree_all_gather(normed_output, "rows")
    height = whole.shape[0]
    cols = whole.shape[1]
    flat = whole.reshape(-1, chans)
    pre = jnp.dot(flat, columns, preferred_element_type=jnp.float32) + up_bias
    post = jax.nn.gelu(pre, approximate=False)
    norms = jnp.sqrt(jnp.sum(post * post, axis=0) + 1e-06)
    cot_f = grad_out[0].reshape(flat.shape[0], -1).astype(jnp.float32)
    dnorm = grn_gamma * jnp.sum(cot_f * post, axis=0)
    norm_total = lax.psum(jnp.sum(norms), "rows")
    denom = norm_total / FF + 1e-06
    ratio = norms / denom
    output = (grn_gamma * (post * ratio) + grn_beta + post).astype(jnp.bfloat16)
    cross = lax.psum(jnp.sum(dnorm * norms), "rows")
    dnorms = dnorm / denom - cross / (denom * denom) / FF
    dpost = cot_f * (1.0 + grn_gamma * ratio) + post * (dnorms / norms)
    dpre = (dpost * gelu_grad(pre)).astype(jnp.bfloat16)
    w_term = lax.dot_general(
        flat, dpre, (((0,), (0,)), ((), ())), preferred_element_type=jnp.float32
    )
    n_fsdp = lax.axis_size("fsdp")
    up_grad = ring_reduce_scatter(
        w_term.astype(jnp.bfloat16).reshape((n_fsdp, chans // n_fsdp, -1)), "fsdp", ring
    )
    dpre_rows = dpre.reshape(height, cols, -1)
    group_terms = jnp.einsum(
        "hwf,cf->hwc", dpre_rows, columns, preferred_element_type=jnp.float32
    ).astype(jnp.bfloat16)
    n_rows = lax.axis_size("rows")
    normed_input_gradient = tree_reduce_scatter(
        group_terms.reshape((n_rows, height // n_rows) + group_terms.shape[1:]), "rows"
    )
    activation_gradient = layer_norm_backward(
        normed_input_gradient, layer_norm_weight, standardized_input, inverse_deviation
    )
    grad_pad = extended(activation_gradient, (("rows", 0),), 3)
    dframe = back_conv(grad_pad, kernel).astype(jnp.bfloat16)
    kernel_local = kern_grad(padded, activation_gradient)
    n_rows = lax.axis_size("rows")
    kernel_part = tree_reduce_scatter(kernel_local.reshape(n_rows, -1), "rows")
    kernel_total = tree_all_gather(lax.psum(kernel_part, "fsdp"), "rows").reshape(
        kernel_local.shape
    )
    activation = output.reshape(1, height, cols, -1)
    return (activation, dframe.reshape((1,) + dframe.shape), up_grad, kernel_total)


def solution(mesh):
    placed = (
        P("fsdp", "rows", None, None),
        P(),
        P(),
        P(),
        P(),
        P("fsdp", "rows"),
        P("rows"),
        P("rows"),
        P("rows"),
        P("fsdp", None, None, "rows"),
    )
    return jax.shard_map(
        functools.partial(body, fsdp_ring(mesh)),
        mesh=mesh,
        in_specs=placed,
        out_specs=(
            P("fsdp", None, None, "rows"),
            P("fsdp", "rows", None, None),
            P("fsdp", "rows"),
            P(),
        ),
        check_vma=False,
    )
```

profile of v0, /device:TPU:0, one launch (start us, length us, event | category | flops | bytes accessed | tf_op | source)
XLA Modules:
  0.0 275.6 jit_solution(5724363738028582769)
XLA Ops:
  7.2 3.1 %collective-permute-start = (bf16[192,1536]{1,0:T(8,128)(2,1)}, bf16[192,1536]{1,0:T(8,128)(2,1)S(1)}, u32[]{:S(2)}, u32[]{:S(2)}) collective-permute-start(bf16[192,1536]{1,0:T(8,128)(2,1)} %param.19), channel_id=1, source_target_pairs={{0,8},{8,16},{16,24},{24,28},{28,20},{20,12},{12,4},{4,0},{1,9},{9... | collective-permute-start | bytes 1769480 | tf_op jit(solution)/shard_map/ppermute | solution.py:111
  10.3 1.2 dynamic_slice.96
  22.8 2.0 fusion.160
  33.7 1.7 slice_reduce_fusion.48
  35.4 1.8 slice_reduce_fusion.47
  41.8 1.4 slice_reduce_fusion.46
  43.3 0.4 broadcast_in_dim.49
  43.7 0.6 copy-done.3
  44.4 0.8 copy-done.2
  45.3 1.5 collective-permute-start.2
  46.8 1.3 collective-permute-start.3
  48.1 1.9 collective-permute-start.6
  50.2 1.8 collective-permute-done.3
  52.5 3.4 %fusion.158 = (f32[3,16]{1,0:T(4,128)S(1)}, f32[3,16,1536]{2,1,0:T(8,128)S(1)}) fusion(f32[1536]{0:T(1024)S(1)} %get-tuple-element.105, bf16[9,22,1536]{2,1,0:T(8,128)(2,1)S(1)} %select_maximum_fusion.2, f32[1536]{0:T(1024)S(1)} %get-tuple-element.106, f32[1536]{0:T(1024)S(1)} %get-tuple-element.59, f32[1536]{0:T(1024)S(1)} %get-tuple-element.60, ...), kind=kLoop, calls=%fused_computation.380 | loop fusion | flops 10911696 | bytes 7827648 | tf_op jit(solution)/shard_map/reduce_sum | solution.py:215
  56.3 4.1 %collective-permute-start.4 = (bf16[1,3,16,1536]{3,2,1,0:T(8,128)(2,1)S(1)}, bf16[1,3,16,1536]{3,2,1,0:T(8,128)(2,1)S(1)}, u32[]{:S(2)}, u32[]{:S(2)}) collective-permute-start(bf16[1,3,16,1536]{3,2,1,0:T(8,128)(2,1)S(1)} %fusion.149), channel_id=1, source_target_pairs={{0,1},{1,0},{2,3},{3,2},{4,5},{5,4},{6,7},{7,6},{8,9},{9,8},{10,11... | collective-permute-start | bytes 442376 | tf_op jit(solution)/shard_map/ppermute | solution.py:169
  60.4 1.0 collective-permute-done.4
  61.5 0.6 collective-permute-done.6
  62.1 2.1 collective-permute-start.8
  64.6 6.1 %collective-permute-done.5 = bf16[2,3,16,1536]{3,2,1,0:T(8,128)(2,1)S(1)} collective-permute-done((bf16[2,3,16,1536]{3,2,1,0:T(8,128)(2,1)S(1)}, bf16[2,3,16,1536]{3,2,1,0:T(8,128)(2,1)S(1)}, u32[]{:S(2)}, u32[]{:S(2)}) %collective-permute-start.5) | collective-permute-done | bytes 294944 | tf_op jit(solution)/shard_map/ppermute | solution.py:169
  70.8 6.2 %collective-permute-done.8 = bf16[192,1536]{1,0:T(8,128)(2,1)S(1)} collective-permute-done((bf16[192,1536]{1,0:T(8,128)(2,1)S(1)}, bf16[192,1536]{1,0:T(8,128)(2,1)S(1)}, u32[]{:S(2)}, u32[]{:S(2)}) %collective-permute-start.8) | collective-permute-done | bytes 589856 | tf_op jit(solution)/shard_map/ppermute | solution.py:111
  77.0 2.4 collective-permute-start.10
  79.5 0.4 collective-permute-done.9
  80.0 13.7 %collective-permute-done.10 = bf16[192,1536]{1,0:T(8,128)(2,1)S(1)} collective-permute-done((bf16[192,1536]{1,0:T(8,128)(2,1)S(1)}, bf16[192,1536]{1,0:T(8,128)(2,1)S(1)}, u32[]{:S(2)}, u32[]{:S(2)}) %collective-permute-start.10) | collective-permute-done | bytes 589856 | tf_op jit(solution)/shard_map/ppermute | solution.py:111
  93.8 4.8 %fusion.4 = (f32[1536]{0:T(1024)S(1)}, f32[1536]{0:T(1024)S(1)}, f32[192,1536]{1,0:T(8,128)}, f32[192,1536]{1,0:T(8,128)}) fusion(bf16[1,12,16,1536]{3,2,1,0:T(8,128)(2,1)S(1)} %copy-done.4, f32[1536]{0:T(1024)S(1)} %copy-done.44, bf16[192,1536]{1,0:T(8,128)(2,1)S(1)} %bitcast.106, bf16[1536,1536]{1,0:T(8,128)(2,1)S(1)} %bitcast.104), kind=kOutput, calls=%fused_computation.63 | convolution fusion | flops 926610432 | bytes 8275968 | tf_op jit(solution)/shard_map/dot_general | solution.py:272
  98.6 0.6 multiply_reduce_fusion.3
  99.2 6.4 %all-reduce.2 = (f32[]{:T(128)}, f32[]{:T(128)}) all-reduce(f32[]{:T(128)} %get-tuple-element.117, f32[]{:T(128)} %get-tuple-element.116), channel_id=1, replica_groups=mesh['fsdp'=8,'rows'=4] {'rows'}, use_global_device_ids=true, to_apply=%region_4.5 | all-reduce | flops 2 | bytes 16 | tf_op jit(solution)/shard_map/psum | solution.py:277
  106.9 3.4 %fusion.3 = (bf16[192,1536]{1,0:T(8,128)(2,1)S(1)}, bf16[192,1536]{1,0:T(8,128)(2,1)}) fusion(f32[192,1536]{1,0:T(8,128)} %get-tuple-element.155, f32[192,1536]{1,0:T(8,128)} %get-tuple-element.124, bf16[1,12,16,1536]{3,2,1,0:T(8,128)(2,1)} %param.23, f32[1536]{0:T(1024)S(1)} %get-tuple-element.139, f32[1536]{0:T(1024)S(1)} %get-tuple-element.122, ...), kind=kLoop, calls=%fused_computation.62 | loop fusion | flops 5603328 | bytes 4159488 | tf_op jit(solution)/shard_map/convert_element_type | solution.py:284
  110.3 4.0 %convolution_convert_fusion.1 = bf16[12,16,1536]{2,1,0:T(8,128)(2,1)S(1)} fusion(bf16[12,16,1536]{2,1,0:T(8,128)(2,1)S(1)} %bitcast.108, bf16[1536,1536,1]{1,0,2:T(8,128)(2,1)} %bitcast.105), kind=kOutput, calls=%fused_computation.52 | convolution fusion | flops 906264576 | bytes 5898240 | tf_op jit(solution)/shard_map/hwf,cf->hwc/dot_general | solution.py:293
  114.4 0.8 copy-done.5
  115.2 0.7 dynamic-slice_bitcast_fusion.2
  130.7 1.1 convert_add_fusion.6
  131.9 1.7 collective-permute-start.12
  133.6 1.4 convolution_convert_fusion
  135.1 1.0 dynamic-slice_bitcast_fusion.1
  136.1 1.8 collective-permute-start.18
  138.1 3.3 %collective-permute-done.12 = f32[1,3,16,1536]{3,2,1,0:T(8,128)S(1)} collective-permute-done((f32[1,3,16,1536]{3,2,1,0:T(8,128)S(1)}, f32[1,3,16,1536]{3,2,1,0:T(8,128)S(1)}, u32[]{:S(2)}, u32[]{:S(2)}) %collective-permute-start.12) | collective-permute-done | bytes 294944 | tf_op jit(solution)/shard_map/ppermute | solution.py:68
  141.6 0.9 fusion.146
  142.5 0.8 fusion.147
  143.3 1.7 collective-permute-start.13
  145.0 1.3 collective-permute-start.14
  146.3 0.6 fusion.145
  147.6 0.5 stack.199
  148.8 2.6 collective-permute-start.22
  151.4 0.6 collective-permute-done.18
  151.9 2.2 fusion.13
  154.2 1.8 collective-permute-start.19
  156.1 1.2 collective-permute-start.23
  157.6 3.0 %collective-permute-done.23 = f32[1,18816]{1,0:T(1,128)S(1)} collective-permute-done((f32[1,18816]{1,0:T(1,128)S(1)}, f32[1,18816]{1,0:T(1,128)S(1)}, u32[]{:S(2)}, u32[]{:S(2)}) %collective-permute-start.23) | collective-permute-done | bytes 75296 | tf_op jit(solution)/shard_map/ppermute | solution.py:68
  160.5 0.7 dynamic-slice_add_fusion
  161.4 3.7 %fusion.152 = bf16[1,3,16,1536]{3,2,1,0:T(8,128)(2,1)} fusion(f32[1536]{0:T(1024)} %copy-done.33, bf16[9,22,1536]{2,1,0:T(8,128)(2,1)S(1)} %select_maximum_fusion, f32[1536]{0:T(1024)} %copy-done.34, f32[1536]{0:T(1024)S(1)} %get-tuple-element.59, f32[1536]{0:T(1024)S(1)} %get-tuple-element.60, bf16[3,16,1536]{2,1,0:T(8,128)(2,1)S(1)} %collective-permute-done.13, ...), kind=kLoop, calls=%fused_computation.310 | loop fusion | flops 11132928 | bytes 7084032 | tf_op jit(solution)/shard_map/reshape | solution.py:312
  165.1 65.4 %all-reduce.5.cloned.1.call-done = f32[1,18816]{1,0:T(1,128)} async-done(((f32[1,18816]{1,0:T(1,128)}), f32[1,18816]{1,0:T(1,128)}) %all-reduce.5.cloned.1.call-update) | async-done | bytes 75280 | tf_op jit(solution)/shard_map/psum | solution.py:308
  230.5 1.6 fusion.15
  232.0 1.4 collective-permute-start.16
  233.5 0.7 collective-permute-start.20
  234.4 1.5 collective-permute-start.25
  235.9 11.9 %collective-permute-done.16 = bf16[192,1536]{1,0:T(8,128)(2,1)S(1)} collective-permute-done((bf16[192,1536]{1,0:T(8,128)(2,1)S(1)}, bf16[192,1536]{1,0:T(8,128)(2,1)S(1)}, u32[]{:S(2)}, u32[]{:S(2)}) %collective-permute-start.16) | collective-permute-done | bytes 589856 | tf_op jit(solution)/shard_map/ppermute | solution.py:146
  247.8 1.1 collective-permute-done.20
  248.9 1.5 fusion.14
  250.4 1.7 collective-permute-start.17
  252.1 0.4 collective-permute-start.21
  252.7 0.9 select_n.320
  253.6 11.5 %collective-permute-done.17 = bf16[192,1536]{1,0:T(8,128)(2,1)S(1)} collective-permute-done((bf16[192,1536]{1,0:T(8,128)(2,1)S(1)}, bf16[192,1536]{1,0:T(8,128)(2,1)S(1)}, u32[]{:S(2)}, u32[]{:S(2)}) %collective-permute-start.17) | collective-permute-done | bytes 589856 | tf_op jit(solution)/shard_map/ppermute | solution.py:146
  265.1 1.4 collective-permute-done.21
  266.4 2.3 fusion.16
  (187 shorter events, 4.1 us)
Async XLA Ops:
  7.2 223.3 %all-reduce.5.cloned.1.call-start = ((), (), s32[]{:S(2)}) async-start(), calls=%async_computation | async-start | bytes 150528 | tf_op jit(solution)/shard_map/psum | solution.py:308
  7.2 37.2 %collective-permute-start = (bf16[192,1536]{1,0:T(8,128)(2,1)}, bf16[192,1536]{1,0:T(8,128)(2,1)S(1)}, u32[]{:S(2)}, u32[]{:S(2)}) collective-permute-start(bf16[192,1536]{1,0:T(8,128)(2,1)} %param.19), channel_id=1, source_target_pairs={{0,8},{8,16},{16,24},{24,28},{28,20},{20,12},{12,4},{4,0},{1,9},{9... | collective-permute-start | bytes 1769480 | tf_op jit(solution)/shard_map/ppermute | solution.py:111
  10.3 34.2 %collective-permute-start.1 = (bf16[192,1536]{1,0:T(8,128)(2,1)}, bf16[192,1536]{1,0:T(8,128)(2,1)S(1)}, u32[]{:S(2)}, u32[]{:S(2)}) collective-permute-start(bf16[192,1536]{1,0:T(8,128)(2,1)} %param.19), channel_id=1, source_target_pairs={{0,4},{8,0},{16,8},{24,16},{28,24},{20,28},{12,20},{4,12},{1,5},{9... | collective-permute-start | bytes 1769480 | tf_op jit(solution)/shard_map/ppermute | solution.py:113
  37.2 15.0 %copy-start.8 = (f32[1536]{0:T(1024)}, f32[1536]{0:T(1024)S(1)}, u32[]{:S(2)}) copy-start(f32[1536]{0:T(1024)S(1)} %get-tuple-element.87) | copy-start | bytes 18436
  37.2 15.0 %copy-start.10 = (f32[1536]{0:T(1024)}, f32[1536]{0:T(1024)S(1)}, u32[]{:S(2)}) copy-start(f32[1536]{0:T(1024)S(1)} %get-tuple-element.88) | copy-start | bytes 18436
  37.3 15.0 %copy-start.12 = (f32[1536]{0:T(1024)}, f32[1536]{0:T(1024)S(1)}, u32[]{:S(2)}) copy-start(f32[1536]{0:T(1024)S(1)} %get-tuple-element.89) | copy-start | bytes 18436
  37.3 15.0 %copy-start.14 = (f32[1536]{0:T(1024)}, f32[1536]{0:T(1024)S(1)}, u32[]{:S(2)}) copy-start(f32[1536]{0:T(1024)S(1)} %get-tuple-element.90) | copy-start | bytes 18436
  37.3 15.0 %copy-start.16 = (f32[1536]{0:T(1024)}, f32[1536]{0:T(1024)S(1)}, u32[]{:S(2)}) copy-start(f32[1536]{0:T(1024)S(1)} %get-tuple-element.91) | copy-start | bytes 18436
  37.3 15.0 %copy-start.18 = (f32[1536]{0:T(1024)}, f32[1536]{0:T(1024)S(1)}, u32[]{:S(2)}) copy-start(f32[1536]{0:T(1024)S(1)} %get-tuple-element.92) | copy-start | bytes 18436
  37.3 15.0 %copy-start.20 = (f32[1536]{0:T(1024)}, f32[1536]{0:T(1024)S(1)}, u32[]{:S(2)}) copy-start(f32[1536]{0:T(1024)S(1)} %get-tuple-element.93) | copy-start | bytes 18436
  37.3 15.0 %copy-start.22 = (f32[1536]{0:T(1024)}, f32[1536]{0:T(1024)S(1)}, u32[]{:S(2)}) copy-start(f32[1536]{0:T(1024)S(1)} %get-tuple-element.94) | copy-start | bytes 18436
  37.3 15.0 %copy-start.23 = (f32[1536]{0:T(1024)}, f32[1536]{0:T(1024)S(1)}, u32[]{:S(2)}) copy-start(f32[1536]{0:T(1024)S(1)} %get-tuple-element.95) | copy-start | bytes 18436
  43.2 9.1 %copy-start.24 = (f32[1536]{0:T(1024)}, f32[1536]{0:T(1024)S(1)}, u32[]{:S(2)}) copy-start(f32[1536]{0:T(1024)S(1)} %get-tuple-element.96) | copy-start | bytes 18436
  43.2 9.1 %copy-start.25 = (f32[1536]{0:T(1024)}, f32[1536]{0:T(1024)S(1)}, u32[]{:S(2)}) copy-start(f32[1536]{0:T(1024)S(1)} %get-tuple-element.97) | copy-start | bytes 18436
  43.2 9.1 %copy-start.26 = (f32[1536]{0:T(1024)}, f32[1536]{0:T(1024)S(1)}, u32[]{:S(2)}) copy-start(f32[1536]{0:T(1024)S(1)} %get-tuple-element.98) | copy-start | bytes 18436
  43.2 9.1 %copy-start.27 = (f32[1536]{0:T(1024)}, f32[1536]{0:T(1024)S(1)}, u32[]{:S(2)}) copy-start(f32[1536]{0:T(1024)S(1)} %get-tuple-element.99) | copy-start | bytes 18436
  43.2 9.1 %copy-start.28 = (f32[1536]{0:T(1024)}, f32[1536]{0:T(1024)S(1)}, u32[]{:S(2)}) copy-start(f32[1536]{0:T(1024)S(1)} %get-tuple-element.100) | copy-start | bytes 18436
  43.2 9.1 %copy-start.29 = (f32[1536]{0:T(1024)}, f32[1536]{0:T(1024)S(1)}, u32[]{:S(2)}) copy-start(f32[1536]{0:T(1024)S(1)} %get-tuple-element.101) | copy-start | bytes 18436
  43.3 9.1 %copy-start.30 = (f32[1536]{0:T(1024)}, f32[1536]{0:T(1024)S(1)}, u32[]{:S(2)}) copy-start(f32[1536]{0:T(1024)S(1)} %get-tuple-element.102) | copy-start | bytes 18436
  43.3 9.1 %copy-start.31 = (f32[1536]{0:T(1024)}, f32[1536]{0:T(1024)S(1)}, u32[]{:S(2)}) copy-start(f32[1536]{0:T(1024)S(1)} %get-tuple-element.103) | copy-start | bytes 18436
  43.3 9.1 %copy-start.32 = (f32[1536]{0:T(1024)}, f32[1536]{0:T(1024)S(1)}, u32[]{:S(2)}) copy-start(f32[1536]{0:T(1024)S(1)} %get-tuple-element.104) | copy-start | bytes 18436
  43.3 9.1 %copy-start.33 = (f32[1536]{0:T(1024)}, f32[1536]{0:T(1024)S(1)}, u32[]{:S(2)}) copy-start(f32[1536]{0:T(1024)S(1)} %get-tuple-element.105) | copy-start | bytes 18436
  43.3 9.1 %copy-start.34 = (f32[1536]{0:T(1024)}, f32[1536]{0:T(1024)S(1)}, u32[]{:S(2)}) copy-start(f32[1536]{0:T(1024)S(1)} %get-tuple-element.106) | copy-start | bytes 18436
  45.3 4.9 %collective-permute-start.2 = (bf16[3,16,1536]{2,1,0:T(8,128)(2,1)S(1)}, bf16[3,16,1536]{2,1,0:T(8,128)(2,1)S(1)}, u32[]{:S(2)}, u32[]{:S(2)}) collective-permute-start(bf16[3,16,1536]{2,1,0:T(8,128)(2,1)S(1)} %bitcast.109), channel_id=1, source_target_pairs={{0,1},{1,2},{2,3},{4,5},{5,6},{6,7},{8,9},{9,10},{10,11},{12,13},{... | collective-permute-start | bytes 442376 | tf_op jit(solution)/shard_map/ppermute | solution.py:15
  46.8 5.3 %collective-permute-start.3 = (bf16[3,16,1536]{2,1,0:T(8,128)(2,1)S(1)}, bf16[3,16,1536]{2,1,0:T(8,128)(2,1)S(1)}, u32[]{:S(2)}, u32[]{:S(2)}) collective-permute-start(bf16[3,16,1536]{2,1,0:T(8,128)(2,1)S(1)} %bitcast.110), channel_id=1, source_target_pairs={{1,0},{2,1},{3,2},{5,4},{6,5},{7,6},{9,8},{10,9},{11,10},{13,12},{... | collective-permute-start | bytes 442376 | tf_op jit(solution)/shard_map/ppermute | solution.py:18
  48.1 14.0 %collective-permute-start.6 = (bf16[192,1536]{1,0:T(8,128)(2,1)S(1)}, bf16[192,1536]{1,0:T(8,128)(2,1)S(1)}, u32[]{:S(2)}, u32[]{:S(2)}) collective-permute-start(bf16[192,1536]{1,0:T(8,128)(2,1)S(1)} %collective-permute-done), channel_id=1, source_target_pairs={{0,8},{8,16},{16,24},{24,28},{28,20},{20,12},{12,4},{4,0},{1,9},{9... | collective-permute-start | bytes 1769480 | tf_op jit(solution)/shard_map/ppermute | solution.py:111
  49.9 14.5 %collective-permute-start.7 = (bf16[192,1536]{1,0:T(8,128)(2,1)S(1)}, bf16[192,1536]{1,0:T(8,128)(2,1)S(1)}, u32[]{:S(2)}, u32[]{:S(2)}) collective-permute-start(bf16[192,1536]{1,0:T(8,128)(2,1)S(1)} %collective-permute-done.1), channel_id=1, source_target_pairs={{0,4},{8,0},{16,8},{24,16},{28,24},{20,28},{12,20},{4,12},{1,5},{9... | collective-permute-start | bytes 1769480 | tf_op jit(solution)/shard_map/ppermute | solution.py:113
  55.9 5.4 %copy-start.35 = (f32[3,16]{1,0:T(4,128)}, f32[3,16]{1,0:T(4,128)S(1)}, u32[]{:S(2)}) copy-start(f32[3,16]{1,0:T(4,128)S(1)} %broadcast_multiply_fusion.2) | copy-start | bytes 580
  56.1 5.3 %copy-start.37 = (f32[3,16]{1,0:T(4,128)}, f32[3,16]{1,0:T(4,128)S(1)}, u32[]{:S(2)}) copy-start(f32[3,16]{1,0:T(4,128)S(1)} %add_rsqrt_fusion) | copy-start | bytes 580
  56.3 5.1 %collective-permute-start.4 = (bf16[1,3,16,1536]{3,2,1,0:T(8,128)(2,1)S(1)}, bf16[1,3,16,1536]{3,2,1,0:T(8,128)(2,1)S(1)}, u32[]{:S(2)}, u32[]{:S(2)}) collective-permute-start(bf16[1,3,16,1536]{3,2,1,0:T(8,128)(2,1)S(1)} %fusion.149), channel_id=1, source_target_pairs={{0,1},{1,0},{2,3},{3,2},{4,5},{5,4},{6,7},{7,6},{8,9},{9,8},{10,11... | collective-permute-start | bytes 442376 | tf_op jit(solution)/shard_map/ppermute | solution.py:169
  61.4 9.3 %collective-permute-start.5 = (bf16[2,3,16,1536]{3,2,1,0:T(8,128)(2,1)S(1)}, bf16[2,3,16,1536]{3,2,1,0:T(8,128)(2,1)S(1)}, u32[]{:S(2)}, u32[]{:S(2)}) collective-permute-start(bf16[2,3,16,1536]{3,2,1,0:T(8,128)(2,1)S(1)} %maximum_select_fusion.2), channel_id=1, source_target_pairs={{0,2},{1,3},{2,0},{3,1},{4,6},{5,7},{6,4},{7,5},{8,10},{9,11},{10,... | collective-permute-start | bytes 884744 | tf_op jit(solution)/shard_map/ppermute | solution.py:169
  62.1 14.9 %collective-permute-start.8 = (bf16[192,1536]{1,0:T(8,128)(2,1)S(1)}, bf16[192,1536]{1,0:T(8,128)(2,1)S(1)}, u32[]{:S(2)}, u32[]{:S(2)}) collective-permute-start(bf16[192,1536]{1,0:T(8,128)(2,1)S(1)} %collective-permute-done.6), channel_id=1, source_target_pairs={{0,8},{8,16},{16,24},{24,28},{28,20},{20,12},{12,4},{4,0},{1,9},{9... | collective-permute-start | bytes 1769480 | tf_op jit(solution)/shard_map/ppermute | solution.py:111
  64.5 15.4 %collective-permute-start.9 = (bf16[192,1536]{1,0:T(8,128)(2,1)S(1)}, bf16[192,1536]{1,0:T(8,128)(2,1)S(1)}, u32[]{:S(2)}, u32[]{:S(2)}) collective-permute-start(bf16[192,1536]{1,0:T(8,128)(2,1)S(1)} %collective-permute-done.7), channel_id=1, source_target_pairs={{0,4},{8,0},{16,8},{24,16},{28,24},{20,28},{12,20},{4,12},{1,5},{9... | collective-permute-start | bytes 1769480 | tf_op jit(solution)/shard_map/ppermute | solution.py:113
  77.0 16.7 %collective-permute-start.10 = (bf16[192,1536]{1,0:T(8,128)(2,1)S(1)}, bf16[192,1536]{1,0:T(8,128)(2,1)S(1)}, u32[]{:S(2)}, u32[]{:S(2)}) collective-permute-start(bf16[192,1536]{1,0:T(8,128)(2,1)S(1)} %collective-permute-done.8), channel_id=1, source_target_pairs={{0,8},{8,16},{16,24},{24,28},{28,20},{20,12},{12,4},{4,0},{1,9},{9... | collective-permute-start | bytes 1769480 | tf_op jit(solution)/shard_map/ppermute | solution.py:111
  79.5 14.3 %copy-start.4 = (bf16[1,12,16,1536]{3,2,1,0:T(8,128)(2,1)S(1)}, bf16[1,12,16,1536]{3,2,1,0:T(8,128)(2,1)}, u32[]{:S(2)}) copy-start(bf16[1,12,16,1536]{3,2,1,0:T(8,128)(2,1)} %param.23) | copy-start | bytes 1769476
  79.5 14.3 %copy-start.44 = (f32[1536]{0:T(1024)S(1)}, f32[1536]{0:T(1024)}, u32[]{:S(2)}) copy-start(f32[1536]{0:T(1024)} %param.20) | copy-start | bytes 18436
  93.7 4.9 %copy-start.1 = (bf16[8,192,1536]{2,1,0:T(8,128)(2,1)}, bf16[8,192,1536]{2,1,0:T(8,128)(2,1)S(1)}, u32[]{:S(2)}) copy-start(bf16[8,192,1536]{2,1,0:T(8,128)(2,1)S(1)} %bitcast_dynamic-update-slice_fusion) | copy-start | bytes 14155780
  93.8 13.2 %copy-start.42 = (f32[1536]{0:T(1024)S(1)}, f32[1536]{0:T(1024)}, u32[]{:S(2)}) copy-start(f32[1536]{0:T(1024)} %param.22) | copy-start | bytes 18436
  115.9 14.8 %collective-permute-start.11 = (bf16[2,3,16,1536]{3,2,1,0:T(8,128)(2,1)}, bf16[2,3,16,1536]{3,2,1,0:T(8,128)(2,1)}, u32[]{:S(2)}, u32[]{:S(2)}) collective-permute-start(bf16[2,3,16,1536]{3,2,1,0:T(8,128)(2,1)} %dynamic-slice_bitcast_fusion.2), channel_id=1, source_target_pairs={{0,1},{1,0},{2,3},{3,2},{4,5},{5,4},{6,7},{7,6},{8,9},{9,8},{10,11... | collective-permute-start | bytes 884744 | tf_op jit(solution)/shard_map/ppermute | solution.py:68
  131.9 9.5 %collective-permute-start.12 = (f32[1,3,16,1536]{3,2,1,0:T(8,128)S(1)}, f32[1,3,16,1536]{3,2,1,0:T(8,128)S(1)}, u32[]{:S(2)}, u32[]{:S(2)}) collective-permute-start(f32[1,3,16,1536]{3,2,1,0:T(8,128)S(1)} %constant_dynamic-slice_fusion.3), channel_id=1, source_target_pairs={{0,2},{1,3},{2,0},{3,1},{4,6},{5,7},{6,4},{7,5},{8,10},{9,11},{10,... | collective-permute-start | bytes 884744 | tf_op jit(solution)/shard_map/ppermute | solution.py:68
  135.0 7.5 %copy-start = (bf16[1536,1536]{1,0:T(8,128)(2,1)}, bf16[1536,1536]{1,0:T(8,128)(2,1)S(1)}, u32[]{:S(2)}) copy-start(bf16[1536,1536]{1,0:T(8,128)(2,1)S(1)} %convolution_convert_fusion) | copy-start | bytes 14155780
  135.0 6.3 %copy-start.36 = (f32[3,16]{1,0:T(4,128)S(1)}, f32[3,16]{1,0:T(4,128)}, u32[]{:S(2)}) copy-start(f32[3,16]{1,0:T(4,128)} %copy-done.35) | copy-start | bytes 580
  135.0 6.3 %copy-start.38 = (f32[3,16]{1,0:T(4,128)S(1)}, f32[3,16]{1,0:T(4,128)}, u32[]{:S(2)}) copy-start(f32[3,16]{1,0:T(4,128)} %copy-done.37) | copy-start | bytes 580
  135.0 6.3 %copy-start.40 = (f32[1536]{0:T(1024)S(1)}, f32[1536]{0:T(1024)}, u32[]{:S(2)}) copy-start(f32[1536]{0:T(1024)} %param.17) | copy-start | bytes 18436
  136.1 15.9 %collective-permute-start.18 = (bf16[192,1536]{1,0:T(8,128)(2,1)}, bf16[192,1536]{1,0:T(8,128)(2,1)}, u32[]{:S(2)}, u32[]{:S(2)}) collective-permute-start(bf16[192,1536]{1,0:T(8,128)(2,1)} %get-tuple-element.132), channel_id=1, source_target_pairs={{0,8},{8,16},{16,24},{24,28},{28,20},{20,12},{12,4},{4,0},{1,9},{9... | collective-permute-start | bytes 1769480 | tf_op jit(solution)/shard_map/ppermute | solution.py:144
  137.9 92.6 %collective-permute-start.15 = (bf16[192,1536]{1,0:T(8,128)(2,1)S(1)}, bf16[192,1536]{1,0:T(8,128)(2,1)S(1)}, u32[]{:S(2)}, u32[]{:S(2)}) collective-permute-start(bf16[192,1536]{1,0:T(8,128)(2,1)S(1)} %get-tuple-element.131), channel_id=1, source_target_pairs={{0,4},{8,0},{16,8},{24,16},{28,24},{20,28},{12,20},{4,12},{1,5},{9... | collective-permute-start | bytes 1769480 | tf_op jit(solution)/shard_map/ppermute | solution.py:146
  143.3 14.1 %collective-permute-start.13 = (bf16[3,16,1536]{2,1,0:T(8,128)(2,1)S(1)}, bf16[3,16,1536]{2,1,0:T(8,128)(2,1)S(1)}, u32[]{:S(2)}, u32[]{:S(2)}) collective-permute-start(bf16[3,16,1536]{2,1,0:T(8,128)(2,1)S(1)} %get-tuple-element.120), channel_id=1, source_target_pairs={{0,1},{1,2},{2,3},{4,5},{5,6},{6,7},{8,9},{9,10},{10,11},{12,13},{... | collective-permute-start | bytes 442376 | tf_op jit(solution)/shard_map/ppermute | solution.py:15
  145.0 12.3 %collective-permute-start.14 = (bf16[3,16,1536]{2,1,0:T(8,128)(2,1)S(1)}, bf16[3,16,1536]{2,1,0:T(8,128)(2,1)S(1)}, u32[]{:S(2)}, u32[]{:S(2)}) collective-permute-start(bf16[3,16,1536]{2,1,0:T(8,128)(2,1)S(1)} %get-tuple-element.120), channel_id=1, source_target_pairs={{1,0},{2,1},{3,2},{5,4},{6,5},{7,6},{9,8},{10,9},{11,10},{13,12},{... | collective-permute-start | bytes 442376 | tf_op jit(solution)/shard_map/ppermute | solution.py:18
  148.8 7.2 %collective-permute-start.22 = (f32[2,18816]{1,0:T(2,128)S(1)}, f32[2,18816]{1,0:T(2,128)S(1)}, u32[]{:S(2)}, u32[]{:S(2)}) collective-permute-start(f32[2,18816]{1,0:T(2,128)S(1)} %bitcast.118), channel_id=1, source_target_pairs={{0,1},{1,0},{2,3},{3,2},{4,5},{5,4},{6,7},{7,6},{8,9},{9,8},{10,11... | collective-permute-start | bytes 451592 | tf_op jit(solution)/shard_map/ppermute | solution.py:68
  154.1 7.2 %copy-start.9 = (f32[1536]{0:T(1024)S(1)}, f32[1536]{0:T(1024)}, u32[]{:S(2)}) copy-start(f32[1536]{0:T(1024)} %copy-done.8) | copy-start | bytes 18436
  154.1 7.2 %copy-start.11 = (f32[1536]{0:T(1024)S(1)}, f32[1536]{0:T(1024)}, u32[]{:S(2)}) copy-start(f32[1536]{0:T(1024)} %copy-done.10) | copy-start | bytes 18436
  154.1 7.2 %copy-start.13 = (f32[1536]{0:T(1024)S(1)}, f32[1536]{0:T(1024)}, u32[]{:S(2)}) copy-start(f32[1536]{0:T(1024)} %copy-done.12) | copy-start | bytes 18436
  154.1 7.2 %copy-start.15 = (f32[1536]{0:T(1024)S(1)}, f32[1536]{0:T(1024)}, u32[]{:S(2)}) copy-start(f32[1536]{0:T(1024)} %copy-done.14) | copy-start | bytes 18436
  154.1 7.2 %copy-start.17 = (f32[1536]{0:T(1024)S(1)}, f32[1536]{0:T(1024)}, u32[]{:S(2)}) copy-start(f32[1536]{0:T(1024)} %copy-done.16) | copy-start | bytes 18436
  154.1 7.2 %copy-start.19 = (f32[1536]{0:T(1024)S(1)}, f32[1536]{0:T(1024)}, u32[]{:S(2)}) copy-start(f32[1536]{0:T(1024)} %copy-done.18) | copy-start | bytes 18436
  154.1 7.2 %copy-start.21 = (f32[1536]{0:T(1024)S(1)}, f32[1536]{0:T(1024)}, u32[]{:S(2)}) copy-start(f32[1536]{0:T(1024)} %copy-done.20) | copy-start | bytes 18436
  154.2 76.3 %collective-permute-start.19 = (bf16[192,1536]{1,0:T(8,128)(2,1)}, bf16[192,1536]{1,0:T(8,128)(2,1)S(1)}, u32[]{:S(2)}, u32[]{:S(2)}) collective-permute-start(bf16[192,1536]{1,0:T(8,128)(2,1)} %fusion.13), channel_id=1, source_target_pairs={{0,8},{8,16},{16,24},{24,28},{28,20},{20,12},{12,4},{4,0},{1,9},{9... | collective-permute-start | bytes 1769480 | tf_op jit(solution)/shard_map/ppermute | solution.py:144
  156.1 4.4 %collective-permute-start.23 = (f32[1,18816]{1,0:T(1,128)S(1)}, f32[1,18816]{1,0:T(1,128)S(1)}, u32[]{:S(2)}, u32[]{:S(2)}) collective-permute-start(f32[1,18816]{1,0:T(1,128)S(1)} %constant_dynamic-slice_fusion), channel_id=1, source_target_pairs={{0,2},{1,3},{2,0},{3,1},{4,6},{5,7},{6,4},{7,5},{8,10},{9,11},{10,... | collective-permute-start | bytes 225800 | tf_op jit(solution)/shard_map/ppermute | solution.py:68
  230.4 3.7 %collective-permute-start.24 = (f32[1,18816]{1,0:T(1,128)}, f32[1,18816]{1,0:T(1,128)S(1)}, u32[]{:S(2)}, u32[]{:S(2)}) collective-permute-start(f32[1,18816]{1,0:T(1,128)} %all-reduce.5.cloned.1.call-done), channel_id=1, source_target_pairs={{0,1},{1,0},{2,3},{3,2},{4,5},{5,4},{6,7},{7,6},{8,9},{9,8},{10,11... | collective-permute-start | bytes 225800 | tf_op jit(solution)/shard_map/ppermute | solution.py:169
  232.0 15.8 %collective-permute-start.16 = (bf16[192,1536]{1,0:T(8,128)(2,1)S(1)}, bf16[192,1536]{1,0:T(8,128)(2,1)S(1)}, u32[]{:S(2)}, u32[]{:S(2)}) collective-permute-start(bf16[192,1536]{1,0:T(8,128)(2,1)S(1)} %get-tuple-element.129), channel_id=1, source_target_pairs={{0,4},{8,0},{16,8},{24,16},{28,24},{20,28},{12,20},{4,12},{1,5},{9... | collective-permute-start | bytes 1769480 | tf_op jit(solution)/shard_map/ppermute | solution.py:146
  233.5 15.4 %collective-permute-start.20 = (bf16[192,1536]{1,0:T(8,128)(2,1)S(1)}, bf16[192,1536]{1,0:T(8,128)(2,1)S(1)}, u32[]{:S(2)}, u32[]{:S(2)}) collective-permute-start(bf16[192,1536]{1,0:T(8,128)(2,1)S(1)} %get-tuple-element.130), channel_id=1, source_target_pairs={{0,8},{8,16},{16,24},{24,28},{28,20},{20,12},{12,4},{4,0},{1,9},{9... | collective-permute-start | bytes 1769480 | tf_op jit(solution)/shard_map/ppermute | solution.py:144
  234.4 18.1 %collective-permute-start.25 = (f32[2,18816]{1,0:T(2,128)S(1)}, f32[2,18816]{1,0:T(2,128)S(1)}, u32[]{:S(2)}, u32[]{:S(2)}) collective-permute-start(f32[2,18816]{1,0:T(2,128)S(1)} %maximum_select_fusion.3), channel_id=1, source_target_pairs={{0,2},{1,3},{2,0},{3,1},{4,6},{5,7},{6,4},{7,5},{8,10},{9,11},{10,... | collective-permute-start | bytes 451592 | tf_op jit(solution)/shard_map/ppermute | solution.py:169
  250.4 14.6 %collective-permute-start.17 = (bf16[192,1536]{1,0:T(8,128)(2,1)S(1)}, bf16[192,1536]{1,0:T(8,128)(2,1)S(1)}, u32[]{:S(2)}, u32[]{:S(2)}) collective-permute-start(bf16[192,1536]{1,0:T(8,128)(2,1)S(1)} %get-tuple-element.127), channel_id=1, source_target_pairs={{0,4},{8,0},{16,8},{24,16},{28,24},{20,28},{12,20},{4,12},{1,5},{9... | collective-permute-start | bytes 1769480 | tf_op jit(solution)/shard_map/ppermute | solution.py:146
  252.1 14.3 %collective-permute-start.21 = (bf16[192,1536]{1,0:T(8,128)(2,1)S(1)}, bf16[192,1536]{1,0:T(8,128)(2,1)S(1)}, u32[]{:S(2)}, u32[]{:S(2)}) collective-permute-start(bf16[192,1536]{1,0:T(8,128)(2,1)S(1)} %get-tuple-element.128), channel_id=1, source_target_pairs={{0,8},{8,16},{16,24},{24,28},{28,20},{20,12},{12,4},{4,0},{1,9},{9... | collective-permute-start | bytes 1769480 | tf_op jit(solution)/shard_map/ppermute | solution.py:144
  (8 other events, 20.9 us)
Sparse Core Ops, SparseCore 0:
  161.4 68.9 all-reduce.4
where the time goes:
time: 277 us; the launch traced here: 276 us
  waiting for transfers between devices  128 us (46%)
  between operations  56.1 us (20%)
  starting transfers between devices  34.7 us (13%)
  other arithmetic  24.5 us (9%)
  local copies, waits for them, and re-layouts  15.5 us (6%)
  matrix products  10.3 us (4%)
  blocking collectives  6.37 us (2%)
    psum x1, waiting for transfers between devices, body(): lax.psum(kernel_part, 'fsdp')  65.4 us
    ppermute x3, waiting for transfers between devices, ring_reduce_scatter(): ccw = lax.ppermute(ccw, axis, backward)  23.4 us
    ppermute x4, waiting for transfers between devices, ring_all_gather(): cw = lax.ppermute(cw, axis, forward)  20.5 us
    ppermute x4, starting transfers between devices, ring_all_gather(): cw = lax.ppermute(cw, axis, forward)  9.53 us
    ppermute x4, waiting for transfers between devices, tree_all_gather(): other = lax.ppermute(data, axis, perm)  7.08 us
    psum x1, blocking collectives, body(): norm_total = lax.psum(jnp.sum(norms), 'rows')  6.37 us
    ppermute x4, waiting for transfers between devices, tree_reduce_scatter(): lax.ppermute(give, axis, perm).astype(jnp.float32)  6.24 us
    ppermute x4, starting transfers between devices, tree_all_gather(): other = lax.ppermute(data, axis, perm)  5.65 us
  transfers between devices with their start and end apart: 27, of which 16 were waited for; matrix products, arithmetic and copies ran while one was open for 11% of the time, Pallas kernels for 0%

commit v1 on v0

--- a/solution.py
+++ b/solution.py
@@ -305,9 +305,9 @@
     kernel_local = kern_grad(padded, activation_gradient)
     n_rows = lax.axis_size("rows")
     kernel_part = tree_reduce_scatter(kernel_local.reshape(n_rows, -1), "rows")
-    kernel_total = tree_all_gather(lax.psum(kernel_part, "fsdp"), "rows").reshape(
-        kernel_local.shape
-    )
+    kernel_total = tree_all_gather(
+        jnp.sum(lax.all_gather(kernel_part, "fsdp"), axis=0), "rows"
+    ).reshape(kernel_local.shape)
     activation = output.reshape(1, height, cols, -1)
     return (activation, dframe.reshape((1,) + dframe.shape), up_grad, kernel_total)
 

time: 277 us -> 229 us (0.83)
  waiting for transfers between devices: 128 us -> 57.3 us
  blocking collectives: 6.37 us -> 41.2 us
  between operations: 56.1 us -> 43.8 us
    psum x1 -> x0, waiting for transfers between devices: 65.4 us -> none  [body(): lax.psum(kernel_part, 'fsdp')]
    all_gather x0 -> x1, blocking collectives: none -> 34.8 us  [body(): lax.all_gather(kernel_part, 'fsdp')]
    ppermute x4, waiting for transfers between devices: 6.24 us -> 3.26 us  [tree_reduce_scatter(): lax.ppermute(give, axis, perm).astype(jnp.float32)]
  transfers between devices with their start and end apart: 27 -> 26, of which waited for: 16 -> 14; matrix products, arithmetic and copies ran while one was open for 11% -> 13% of each run, Pallas kernels for 0% -> 0%
where the time goes in v1:
time: 229 us; the launch traced here: 228 us
  waiting for transfers between devices  57.3 us (25%)
  between operations  43.8 us (19%)
  blocking collectives  41.2 us (18%)
  starting transfers between devices  35.5 us (16%)
  other arithmetic  24.3 us (11%)
  local copies, waits for them, and re-layouts  15.1 us (7%)
  matrix products  10.3 us (4%)
    all_gather x1, blocking collectives, body(): lax.all_gather(kernel_part, 'fsdp')  34.8 us
    ppermute x3, waiting for transfers between devices, ring_reduce_scatter(): ccw = lax.ppermute(ccw, axis, backward)  22.9 us
    ppermute x4, waiting for transfers between devices, ring_all_gather(): cw = lax.ppermute(cw, axis, forward)  20.2 us
    ppermute x4, starting transfers between devices, ring_all_gather(): cw = lax.ppermute(cw, axis, forward)  9.53 us
    ppermute x4, waiting for transfers between devices, tree_all_gather(): other = lax.ppermute(data, axis, perm)  7.24 us
    ppermute x4, starting transfers between devices, ring_reduce_scatter(): cw = lax.ppermute(cw, axis, forward)  7.1 us
    ppermute x4, starting transfers between devices, tree_all_gather(): other = lax.ppermute(data, axis, perm)  6.46 us
    psum x1, blocking collectives, body(): norm_total = lax.psum(jnp.sum(norms), 'rows')  6.43 us
  transfers between devices with their start and end apart: 26, of which 14 were waited for; matrix products, arithmetic and copies ran while one was open for 13% of the time, Pallas kernels for 0%

profile of v1, /device:TPU:0, one launch (start us, length us, event | category | flops | bytes accessed | tf_op | source)
XLA Modules:
  0.0 227.5 jit_solution(4696500118050670771)
XLA Ops:
  0.6 3.1 %collective-permute-start = (bf16[192,1536]{1,0:T(8,128)(2,1)}, bf16[192,1536]{1,0:T(8,128)(2,1)S(1)}, u32[]{:S(2)}, u32[]{:S(2)}) collective-permute-start(bf16[192,1536]{1,0:T(8,128)(2,1)} %param.19), channel_id=1, source_target_pairs={{0,8},{8,16},{16,24},{24,28},{28,20},{20,12},{12,4},{4,0},{1,9},{9... | collective-permute-start | bytes 1769480 | tf_op jit(solution)/shard_map/ppermute | solution.py:111
  3.7 1.2 dynamic_slice.96
  16.2 2.0 fusion.160
  27.2 1.7 slice_reduce_fusion.48
  29.0 1.8 slice_reduce_fusion.47
  35.5 1.4 slice_reduce_fusion.46
  37.0 0.4 broadcast_in_dim.49
  37.4 0.6 copy-done.3
  38.1 0.8 copy-done.2
  39.0 1.5 collective-permute-start.2
  40.4 1.3 collective-permute-start.3
  41.7 1.9 collective-permute-start.6
  43.9 1.8 collective-permute-done.3
  46.3 3.4 %fusion.158 = (f32[3,16]{1,0:T(4,128)S(1)}, f32[3,16,1536]{2,1,0:T(8,128)S(1)}) fusion(f32[1536]{0:T(1024)S(1)} %get-tuple-element.105, bf16[9,22,1536]{2,1,0:T(8,128)(2,1)S(1)} %select_maximum_fusion.2, f32[1536]{0:T(1024)S(1)} %get-tuple-element.106, f32[1536]{0:T(1024)S(1)} %get-tuple-element.59, f32[1536]{0:T(1024)S(1)} %get-tuple-element.60, ...), kind=kLoop, calls=%fused_computation.380 | loop fusion | flops 10911696 | bytes 7827648 | tf_op jit(solution)/shard_map/reduce_sum | solution.py:215
  50.1 4.1 %collective-permute-start.4 = (bf16[1,3,16,1536]{3,2,1,0:T(8,128)(2,1)S(1)}, bf16[1,3,16,1536]{3,2,1,0:T(8,128)(2,1)S(1)}, u32[]{:S(2)}, u32[]{:S(2)}) collective-permute-start(bf16[1,3,16,1536]{3,2,1,0:T(8,128)(2,1)S(1)} %fusion.149), channel_id=1, source_target_pairs={{0,1},{1,0},{2,3},{3,2},{4,5},{5,4},{6,7},{7,6},{8,9},{9,8},{10,11... | collective-permute-start | bytes 442376 | tf_op jit(solution)/shard_map/ppermute | solution.py:169
  54.2 1.0 collective-permute-done.4
  55.3 0.5 collective-permute-done.6
  55.8 2.1 collective-permute-start.8
  57.9 0.3 collective-permute-done.7
  58.3 6.3 %collective-permute-done.5 = bf16[2,3,16,1536]{3,2,1,0:T(8,128)(2,1)S(1)} collective-permute-done((bf16[2,3,16,1536]{3,2,1,0:T(8,128)(2,1)S(1)}, bf16[2,3,16,1536]{3,2,1,0:T(8,128)(2,1)S(1)}, u32[]{:S(2)}, u32[]{:S(2)}) %collective-permute-start.5) | collective-permute-done | bytes 294944 | tf_op jit(solution)/shard_map/ppermute | solution.py:169
  64.7 6.0 %collective-permute-done.8 = bf16[192,1536]{1,0:T(8,128)(2,1)S(1)} collective-permute-done((bf16[192,1536]{1,0:T(8,128)(2,1)S(1)}, bf16[192,1536]{1,0:T(8,128)(2,1)S(1)}, u32[]{:S(2)}, u32[]{:S(2)}) %collective-permute-start.8) | collective-permute-done | bytes 589856 | tf_op jit(solution)/shard_map/ppermute | solution.py:111
  70.7 2.4 %collective-permute-start.10 = (bf16[192,1536]{1,0:T(8,128)(2,1)S(1)}, bf16[192,1536]{1,0:T(8,128)(2,1)S(1)}, u32[]{:S(2)}, u32[]{:S(2)}) collective-permute-start(bf16[192,1536]{1,0:T(8,128)(2,1)S(1)} %collective-permute-done.8), channel_id=1, source_target_pairs={{0,8},{8,16},{16,24},{24,28},{28,20},{20,12},{12,4},{4,0},{1,9},{9... | collective-permute-start | bytes 1769480 | tf_op jit(solution)/shard_map/ppermute | solution.py:111
  73.2 0.4 collective-permute-done.9
  73.6 13.7 %collective-permute-done.10 = bf16[192,1536]{1,0:T(8,128)(2,1)S(1)} collective-permute-done((bf16[192,1536]{1,0:T(8,128)(2,1)S(1)}, bf16[192,1536]{1,0:T(8,128)(2,1)S(1)}, u32[]{:S(2)}, u32[]{:S(2)}) %collective-permute-start.10) | collective-permute-done | bytes 589856 | tf_op jit(solution)/shard_map/ppermute | solution.py:111
  87.5 4.8 %fusion.4 = (f32[1536]{0:T(1024)S(1)}, f32[1536]{0:T(1024)S(1)}, f32[192,1536]{1,0:T(8,128)}, f32[192,1536]{1,0:T(8,128)}) fusion(bf16[1,12,16,1536]{3,2,1,0:T(8,128)(2,1)S(1)} %copy-done.4, f32[1536]{0:T(1024)S(1)} %copy-done.92, bf16[192,1536]{1,0:T(8,128)(2,1)S(1)} %bitcast.108, bf16[1536,1536]{1,0:T(8,128)(2,1)S(1)} %bitcast.106), kind=kOutput, calls=%fused_computation.63 | convolution fusion | flops 926610432 | bytes 8275968 | tf_op jit(solution)/shard_map/dot_general | solution.py:272
  92.3 0.6 multiply_reduce_fusion.3
  92.9 6.4 %all-reduce.2 = (f32[]{:T(128)}, f32[]{:T(128)}) all-reduce(f32[]{:T(128)} %get-tuple-element.117, f32[]{:T(128)} %get-tuple-element.116), channel_id=1, replica_groups=mesh['fsdp'=8,'rows'=4] {'rows'}, use_global_device_ids=true, to_apply=%region_4.5 | all-reduce | flops 2 | bytes 16 | tf_op jit(solution)/shard_map/psum | solution.py:277
  100.7 3.4 %fusion.3 = (bf16[192,1536]{1,0:T(8,128)(2,1)S(1)}, bf16[192,1536]{1,0:T(8,128)(2,1)}) fusion(f32[192,1536]{1,0:T(8,128)} %get-tuple-element.155, f32[192,1536]{1,0:T(8,128)} %get-tuple-element.124, bf16[1,12,16,1536]{3,2,1,0:T(8,128)(2,1)} %param.23, f32[1536]{0:T(1024)S(1)} %get-tuple-element.139, f32[1536]{0:T(1024)S(1)} %get-tuple-element.122, ...), kind=kLoop, calls=%fused_computation.62 | loop fusion | flops 5603328 | bytes 4159488 | tf_op jit(solution)/shard_map/convert_element_type | solution.py:284
  104.1 4.0 %convolution_convert_fusion.1 = bf16[12,16,1536]{2,1,0:T(8,128)(2,1)S(1)} fusion(bf16[12,16,1536]{2,1,0:T(8,128)(2,1)S(1)} %bitcast.110, bf16[1536,1536,1]{1,0,2:T(8,128)(2,1)} %bitcast.107), kind=kOutput, calls=%fused_computation.52 | convolution fusion | flops 906264576 | bytes 5898240 | tf_op jit(solution)/shard_map/hwf,cf->hwc/dot_general | solution.py:293
  108.1 0.8 copy-done.5
  124.0 1.1 convert_add_fusion.6
  125.2 1.7 collective-permute-start.12
  126.9 1.4 convolution_convert_fusion
  128.3 1.0 dynamic-slice_bitcast_fusion.1
  129.3 1.8 collective-permute-start.18
  131.4 3.3 %collective-permute-done.12 = f32[1,3,16,1536]{3,2,1,0:T(8,128)S(1)} collective-permute-done((f32[1,3,16,1536]{3,2,1,0:T(8,128)S(1)}, f32[1,3,16,1536]{3,2,1,0:T(8,128)S(1)}, u32[]{:S(2)}, u32[]{:S(2)}) %collective-permute-start.12) | collective-permute-done | bytes 294944 | tf_op jit(solution)/shard_map/ppermute | solution.py:68
  134.8 0.9 fusion.146
  135.8 0.8 fusion.147
  136.6 1.7 collective-permute-start.13
  138.3 1.3 collective-permute-start.14
  139.6 0.6 fusion.145
  140.9 0.5 stack.199
  141.6 0.3 constant_dynamic-slice_fusion.2
  142.0 2.6 %collective-permute-start.22 = (f32[2,18816]{1,0:T(2,128)S(1)}, f32[2,18816]{1,0:T(2,128)S(1)}, u32[]{:S(2)}, u32[]{:S(2)}) collective-permute-start(f32[2,18816]{1,0:T(2,128)S(1)} %bitcast.120), channel_id=1, source_target_pairs={{0,1},{1,0},{2,3},{3,2},{4,5},{5,4},{6,7},{7,6},{8,9},{9,8},{10,11... | collective-permute-start | bytes 451592 | tf_op jit(solution)/shard_map/ppermute | solution.py:68
  144.6 0.6 collective-permute-done.18
  145.2 1.4 fusion.13
  147.0 1.7 collective-permute-start.19
  148.7 1.1 select_maximum_fusion
  150.1 1.2 collective-permute-start.23
  151.7 3.7 %fusion.152 = bf16[1,3,16,1536]{3,2,1,0:T(8,128)(2,1)} fusion(f32[1536]{0:T(1024)S(1)} %copy-done.80, bf16[9,22,1536]{2,1,0:T(8,128)(2,1)S(1)} %select_maximum_fusion, f32[1536]{0:T(1024)S(1)} %copy-done.82, f32[1536]{0:T(1024)S(1)} %get-tuple-element.59, f32[1536]{0:T(1024)S(1)} %get-tuple-element.60, bf16[3,16,1536]{2,1,0:T(8,128)(2,1)S(1)} %collective-permute-done.13, ...), kind=kLoop, calls=%fused_computation.310 | loop fusion | flops 11132928 | bytes 7084032 | tf_op jit(solution)/shard_map/reshape | solution.py:312
  155.4 34.8 %all-gather = f32[8,1,18816]{2,1,0:T(1,128)S(1)} all-gather(f32[1,1,18816]{2,1,0:T(1,128)S(1)} %add_bitcast_fusion), channel_id=1, replica_groups=mesh['fsdp'=8,'rows'=4] {'fsdp'}, dimensions={0}, use_global_device_ids=true | all-gather | bytes 677376 | tf_op jit(solution)/shard_map/all_gather | solution.py:309
  190.2 0.4 reduce_sum.579
  190.8 1.6 fusion.15
  192.4 0.3 collective-permute-start.16
  192.7 1.8 collective-permute-start.20
  194.7 2.3 collective-permute-start.25
  196.9 11.2 %collective-permute-done.16 = bf16[192,1536]{1,0:T(8,128)(2,1)S(1)} collective-permute-done((bf16[192,1536]{1,0:T(8,128)(2,1)S(1)}, bf16[192,1536]{1,0:T(8,128)(2,1)S(1)}, u32[]{:S(2)}, u32[]{:S(2)}) %collective-permute-start.16) | collective-permute-done | bytes 589856 | tf_op jit(solution)/shard_map/ppermute | solution.py:146
  208.2 1.5 fusion.14
  209.7 0.3 collective-permute-start.17
  210.0 1.8 collective-permute-start.21
  212.0 0.9 select_n.320
  212.9 11.7 %collective-permute-done.17 = bf16[192,1536]{1,0:T(8,128)(2,1)S(1)} collective-permute-done((bf16[192,1536]{1,0:T(8,128)(2,1)S(1)}, bf16[192,1536]{1,0:T(8,128)(2,1)S(1)}, u32[]{:S(2)}, u32[]{:S(2)}) %collective-permute-start.17) | collective-permute-done | bytes 589856 | tf_op jit(solution)/shard_map/ppermute | solution.py:146
  224.6 0.6 collective-permute-done.21
  225.2 2.3 %fusion.16 = f32[192,1536]{1,0:T(8,128)} fusion(bf16[192,1536]{1,0:T(8,128)(2,1)S(1)} %collective-permute-done.21, bf16[192,1536]{1,0:T(8,128)(2,1)S(1)} %collective-permute-done.17, bf16[8,192,1536]{2,1,0:T(8,128)(2,1)} %bitcast.105, s32[]{:T(128)S(6)} %select_n.294), kind=kLoop, calls=%fused_computation.81 | loop fusion | flops 1474560 | bytes 2949124 | tf_op jit(solution)/shard_map/add | solution.py:150
  (283 shorter events, 3.9 us)
Async XLA Ops:
  0.6 37.5 %collective-permute-start = (bf16[192,1536]{1,0:T(8,128)(2,1)}, bf16[192,1536]{1,0:T(8,128)(2,1)S(1)}, u32[]{:S(2)}, u32[]{:S(2)}) collective-permute-start(bf16[192,1536]{1,0:T(8,128)(2,1)} %param.19), channel_id=1, source_target_pairs={{0,8},{8,16},{16,24},{24,28},{28,20},{20,12},{12,4},{4,0},{1,9},{9... | collective-permute-start | bytes 1769480 | tf_op jit(solution)/shard_map/ppermute | solution.py:111
  3.7 34.4 %collective-permute-start.1 = (bf16[192,1536]{1,0:T(8,128)(2,1)}, bf16[192,1536]{1,0:T(8,128)(2,1)S(1)}, u32[]{:S(2)}, u32[]{:S(2)}) collective-permute-start(bf16[192,1536]{1,0:T(8,128)(2,1)} %param.19), channel_id=1, source_target_pairs={{0,4},{8,0},{16,8},{24,16},{28,24},{20,28},{12,20},{4,12},{1,5},{9... | collective-permute-start | bytes 1769480 | tf_op jit(solution)/shard_map/ppermute | solution.py:113
  28.9 17.0 %copy-start.7 = (f32[1536]{0:T(1024)}, f32[1536]{0:T(1024)S(1)}, u32[]{:S(2)}) copy-start(f32[1536]{0:T(1024)S(1)} %get-tuple-element.69) | copy-start | bytes 18436
  28.9 17.0 %copy-start.9 = (f32[1536]{0:T(1024)}, f32[1536]{0:T(1024)S(1)}, u32[]{:S(2)}) copy-start(f32[1536]{0:T(1024)S(1)} %get-tuple-element.70) | copy-start | bytes 18436
  28.9 17.0 %copy-start.11 = (f32[1536]{0:T(1024)}, f32[1536]{0:T(1024)S(1)}, u32[]{:S(2)}) copy-start(f32[1536]{0:T(1024)S(1)} %get-tuple-element.71) | copy-start | bytes 18436
  28.9 17.0 %copy-start.13 = (f32[1536]{0:T(1024)}, f32[1536]{0:T(1024)S(1)}, u32[]{:S(2)}) copy-start(f32[1536]{0:T(1024)S(1)} %get-tuple-element.72) | copy-start | bytes 18436
  29.0 17.0 %copy-start.15 = (f32[1536]{0:T(1024)}, f32[1536]{0:T(1024)S(1)}, u32[]{:S(2)}) copy-start(f32[1536]{0:T(1024)S(1)} %get-tuple-element.73) | copy-start | bytes 18436
  29.0 17.0 %copy-start.17 = (f32[1536]{0:T(1024)}, f32[1536]{0:T(1024)S(1)}, u32[]{:S(2)}) copy-start(f32[1536]{0:T(1024)S(1)} %get-tuple-element.74) | copy-start | bytes 18436
  29.0 17.0 %copy-start.19 = (f32[1536]{0:T(1024)}, f32[1536]{0:T(1024)S(1)}, u32[]{:S(2)}) copy-start(f32[1536]{0:T(1024)S(1)} %get-tuple-element.75) | copy-start | bytes 18436
  29.0 17.0 %copy-start.21 = (f32[1536]{0:T(1024)}, f32[1536]{0:T(1024)S(1)}, u32[]{:S(2)}) copy-start(f32[1536]{0:T(1024)S(1)} %get-tuple-element.76) | copy-start | bytes 18436
  30.8 15.2 %copy-start.23 = (f32[1536]{0:T(1024)}, f32[1536]{0:T(1024)S(1)}, u32[]{:S(2)}) copy-start(f32[1536]{0:T(1024)S(1)} %get-tuple-element.77) | copy-start | bytes 18436
  30.8 15.2 %copy-start.25 = (f32[1536]{0:T(1024)}, f32[1536]{0:T(1024)S(1)}, u32[]{:S(2)}) copy-start(f32[1536]{0:T(1024)S(1)} %get-tuple-element.78) | copy-start | bytes 18436
  30.8 15.2 %copy-start.27 = (f32[1536]{0:T(1024)}, f32[1536]{0:T(1024)S(1)}, u32[]{:S(2)}) copy-start(f32[1536]{0:T(1024)S(1)} %get-tuple-element.79) | copy-start | bytes 18436
  30.8 15.2 %copy-start.29 = (f32[1536]{0:T(1024)}, f32[1536]{0:T(1024)S(1)}, u32[]{:S(2)}) copy-start(f32[1536]{0:T(1024)S(1)} %get-tuple-element.80) | copy-start | bytes 18436
  30.8 15.2 %copy-start.31 = (f32[1536]{0:T(1024)}, f32[1536]{0:T(1024)S(1)}, u32[]{:S(2)}) copy-start(f32[1536]{0:T(1024)S(1)} %get-tuple-element.81) | copy-start | bytes 18436
  30.8 15.2 %copy-start.33 = (f32[1536]{0:T(1024)}, f32[1536]{0:T(1024)S(1)}, u32[]{:S(2)}) copy-start(f32[1536]{0:T(1024)S(1)} %get-tuple-element.82) | copy-start | bytes 18436
  30.8 15.2 %copy-start.35 = (f32[1536]{0:T(1024)}, f32[1536]{0:T(1024)S(1)}, u32[]{:S(2)}) copy-start(f32[1536]{0:T(1024)S(1)} %get-tuple-element.83) | copy-start | bytes 18436
  30.9 15.2 %copy-start.37 = (f32[1536]{0:T(1024)}, f32[1536]{0:T(1024)S(1)}, u32[]{:S(2)}) copy-start(f32[1536]{0:T(1024)S(1)} %get-tuple-element.84) | copy-start | bytes 18436
  30.9 15.2 %copy-start.39 = (f32[1536]{0:T(1024)}, f32[1536]{0:T(1024)S(1)}, u32[]{:S(2)}) copy-start(f32[1536]{0:T(1024)S(1)} %get-tuple-element.85) | copy-start | bytes 18436
  30.9 15.2 %copy-start.41 = (f32[1536]{0:T(1024)}, f32[1536]{0:T(1024)S(1)}, u32[]{:S(2)}) copy-start(f32[1536]{0:T(1024)S(1)} %get-tuple-element.86) | copy-start | bytes 18436
  30.9 15.2 %copy-start.43 = (f32[1536]{0:T(1024)}, f32[1536]{0:T(1024)S(1)}, u32[]{:S(2)}) copy-start(f32[1536]{0:T(1024)S(1)} %get-tuple-element.87) | copy-start | bytes 18436
  30.9 15.2 %copy-start.45 = (f32[1536]{0:T(1024)}, f32[1536]{0:T(1024)S(1)}, u32[]{:S(2)}) copy-start(f32[1536]{0:T(1024)S(1)} %get-tuple-element.88) | copy-start | bytes 18436
  30.9 15.2 %copy-start.47 = (f32[1536]{0:T(1024)}, f32[1536]{0:T(1024)S(1)}, u32[]{:S(2)}) copy-start(f32[1536]{0:T(1024)S(1)} %get-tuple-element.89) | copy-start | bytes 18436
  30.9 15.2 %copy-start.49 = (f32[1536]{0:T(1024)}, f32[1536]{0:T(1024)S(1)}, u32[]{:S(2)}) copy-start(f32[1536]{0:T(1024)S(1)} %get-tuple-element.90) | copy-start | bytes 18436
  30.9 15.2 %copy-start.51 = (f32[1536]{0:T(1024)}, f32[1536]{0:T(1024)S(1)}, u32[]{:S(2)}) copy-start(f32[1536]{0:T(1024)S(1)} %get-tuple-element.91) | copy-start | bytes 18436
  30.9 15.2 %copy-start.53 = (f32[1536]{0:T(1024)}, f32[1536]{0:T(1024)S(1)}, u32[]{:S(2)}) copy-start(f32[1536]{0:T(1024)S(1)} %get-tuple-element.92) | copy-start | bytes 18436
  30.9 15.2 %copy-start.55 = (f32[1536]{0:T(1024)}, f32[1536]{0:T(1024)S(1)}, u32[]{:S(2)}) copy-start(f32[1536]{0:T(1024)S(1)} %get-tuple-element.93) | copy-start | bytes 18436
  31.0 15.2 %copy-start.57 = (f32[1536]{0:T(1024)}, f32[1536]{0:T(1024)S(1)}, u32[]{:S(2)}) copy-start(f32[1536]{0:T(1024)S(1)} %get-tuple-element.94) | copy-start | bytes 18436
  31.0 15.2 %copy-start.59 = (f32[1536]{0:T(1024)}, f32[1536]{0:T(1024)S(1)}, u32[]{:S(2)}) copy-start(f32[1536]{0:T(1024)S(1)} %get-tuple-element.95) | copy-start | bytes 18436
  36.9 9.3 %copy-start.61 = (f32[1536]{0:T(1024)}, f32[1536]{0:T(1024)S(1)}, u32[]{:S(2)}) copy-start(f32[1536]{0:T(1024)S(1)} %get-tuple-element.96) | copy-start | bytes 18436
  36.9 9.3 %copy-start.63 = (f32[1536]{0:T(1024)}, f32[1536]{0:T(1024)S(1)}, u32[]{:S(2)}) copy-start(f32[1536]{0:T(1024)S(1)} %get-tuple-element.97) | copy-start | bytes 18436
  36.9 9.3 %copy-start.65 = (f32[1536]{0:T(1024)}, f32[1536]{0:T(1024)S(1)}, u32[]{:S(2)}) copy-start(f32[1536]{0:T(1024)S(1)} %get-tuple-element.98) | copy-start | bytes 18436
  36.9 9.3 %copy-start.67 = (f32[1536]{0:T(1024)}, f32[1536]{0:T(1024)S(1)}, u32[]{:S(2)}) copy-start(f32[1536]{0:T(1024)S(1)} %get-tuple-element.99) | copy-start | bytes 18436
  36.9 9.3 %copy-start.69 = (f32[1536]{0:T(1024)}, f32[1536]{0:T(1024)S(1)}, u32[]{:S(2)}) copy-start(f32[1536]{0:T(1024)S(1)} %get-tuple-element.100) | copy-start | bytes 18436
  36.9 9.3 %copy-start.71 = (f32[1536]{0:T(1024)}, f32[1536]{0:T(1024)S(1)}, u32[]{:S(2)}) copy-start(f32[1536]{0:T(1024)S(1)} %get-tuple-element.101) | copy-start | bytes 18436
  36.9 9.3 %copy-start.73 = (f32[1536]{0:T(1024)}, f32[1536]{0:T(1024)S(1)}, u32[]{:S(2)}) copy-start(f32[1536]{0:T(1024)S(1)} %get-tuple-element.102) | copy-start | bytes 18436
  37.0 9.3 %copy-start.75 = (f32[1536]{0:T(1024)}, f32[1536]{0:T(1024)S(1)}, u32[]{:S(2)}) copy-start(f32[1536]{0:T(1024)S(1)} %get-tuple-element.103) | copy-start | bytes 18436
  39.0 4.9 %collective-permute-start.2 = (bf16[3,16,1536]{2,1,0:T(8,128)(2,1)S(1)}, bf16[3,16,1536]{2,1,0:T(8,128)(2,1)S(1)}, u32[]{:S(2)}, u32[]{:S(2)}) collective-permute-start(bf16[3,16,1536]{2,1,0:T(8,128)(2,1)S(1)} %bitcast.111), channel_id=1, source_target_pairs={{0,1},{1,2},{2,3},{4,5},{5,6},{6,7},{8,9},{9,10},{10,11},{12,13},{... | collective-permute-start | bytes 442376 | tf_op jit(solution)/shard_map/ppermute | solution.py:15
  40.4 5.3 %collective-permute-start.3 = (bf16[3,16,1536]{2,1,0:T(8,128)(2,1)S(1)}, bf16[3,16,1536]{2,1,0:T(8,128)(2,1)S(1)}, u32[]{:S(2)}, u32[]{:S(2)}) collective-permute-start(bf16[3,16,1536]{2,1,0:T(8,128)(2,1)S(1)} %bitcast.112), channel_id=1, source_target_pairs={{1,0},{2,1},{3,2},{5,4},{6,5},{7,6},{9,8},{10,9},{11,10},{13,12},{... | collective-permute-start | bytes 442376 | tf_op jit(solution)/shard_map/ppermute | solution.py:18
  41.7 14.0 %collective-permute-start.6 = (bf16[192,1536]{1,0:T(8,128)(2,1)S(1)}, bf16[192,1536]{1,0:T(8,128)(2,1)S(1)}, u32[]{:S(2)}, u32[]{:S(2)}) collective-permute-start(bf16[192,1536]{1,0:T(8,128)(2,1)S(1)} %collective-permute-done), channel_id=1, source_target_pairs={{0,8},{8,16},{16,24},{24,28},{28,20},{20,12},{12,4},{4,0},{1,9},{9... | collective-permute-start | bytes 1769480 | tf_op jit(solution)/shard_map/ppermute | solution.py:111
  43.6 14.5 %collective-permute-start.7 = (bf16[192,1536]{1,0:T(8,128)(2,1)S(1)}, bf16[192,1536]{1,0:T(8,128)(2,1)S(1)}, u32[]{:S(2)}, u32[]{:S(2)}) collective-permute-start(bf16[192,1536]{1,0:T(8,128)(2,1)S(1)} %collective-permute-done.1), channel_id=1, source_target_pairs={{0,4},{8,0},{16,8},{24,16},{28,24},{20,28},{12,20},{4,12},{1,5},{9... | collective-permute-start | bytes 1769480 | tf_op jit(solution)/shard_map/ppermute | solution.py:113
  50.1 5.1 %collective-permute-start.4 = (bf16[1,3,16,1536]{3,2,1,0:T(8,128)(2,1)S(1)}, bf16[1,3,16,1536]{3,2,1,0:T(8,128)(2,1)S(1)}, u32[]{:S(2)}, u32[]{:S(2)}) collective-permute-start(bf16[1,3,16,1536]{3,2,1,0:T(8,128)(2,1)S(1)} %fusion.149), channel_id=1, source_target_pairs={{0,1},{1,0},{2,3},{3,2},{4,5},{5,4},{6,7},{7,6},{8,9},{9,8},{10,11... | collective-permute-start | bytes 442376 | tf_op jit(solution)/shard_map/ppermute | solution.py:169
  55.2 9.3 %collective-permute-start.5 = (bf16[2,3,16,1536]{3,2,1,0:T(8,128)(2,1)S(1)}, bf16[2,3,16,1536]{3,2,1,0:T(8,128)(2,1)S(1)}, u32[]{:S(2)}, u32[]{:S(2)}) collective-permute-start(bf16[2,3,16,1536]{3,2,1,0:T(8,128)(2,1)S(1)} %maximum_select_fusion.2), channel_id=1, source_target_pairs={{0,2},{1,3},{2,0},{3,1},{4,6},{5,7},{6,4},{7,5},{8,10},{9,11},{10,... | collective-permute-start | bytes 884744 | tf_op jit(solution)/shard_map/ppermute | solution.py:169
  55.8 14.9 %collective-permute-start.8 = (bf16[192,1536]{1,0:T(8,128)(2,1)S(1)}, bf16[192,1536]{1,0:T(8,128)(2,1)S(1)}, u32[]{:S(2)}, u32[]{:S(2)}) collective-permute-start(bf16[192,1536]{1,0:T(8,128)(2,1)S(1)} %collective-permute-done.6), channel_id=1, source_target_pairs={{0,8},{8,16},{16,24},{24,28},{28,20},{20,12},{12,4},{4,0},{1,9},{9... | collective-permute-start | bytes 1769480 | tf_op jit(solution)/shard_map/ppermute | solution.py:111
  58.2 15.4 %collective-permute-start.9 = (bf16[192,1536]{1,0:T(8,128)(2,1)S(1)}, bf16[192,1536]{1,0:T(8,128)(2,1)S(1)}, u32[]{:S(2)}, u32[]{:S(2)}) collective-permute-start(bf16[192,1536]{1,0:T(8,128)(2,1)S(1)} %collective-permute-done.7), channel_id=1, source_target_pairs={{0,4},{8,0},{16,8},{24,16},{28,24},{20,28},{12,20},{4,12},{1,5},{9... | collective-permute-start | bytes 1769480 | tf_op jit(solution)/shard_map/ppermute | solution.py:113
  70.7 16.7 %collective-permute-start.10 = (bf16[192,1536]{1,0:T(8,128)(2,1)S(1)}, bf16[192,1536]{1,0:T(8,128)(2,1)S(1)}, u32[]{:S(2)}, u32[]{:S(2)}) collective-permute-start(bf16[192,1536]{1,0:T(8,128)(2,1)S(1)} %collective-permute-done.8), channel_id=1, source_target_pairs={{0,8},{8,16},{16,24},{24,28},{28,20},{20,12},{12,4},{4,0},{1,9},{9... | collective-permute-start | bytes 1769480 | tf_op jit(solution)/shard_map/ppermute | solution.py:111
  73.1 14.3 %copy-start.4 = (bf16[1,12,16,1536]{3,2,1,0:T(8,128)(2,1)S(1)}, bf16[1,12,16,1536]{3,2,1,0:T(8,128)(2,1)}, u32[]{:S(2)}) copy-start(bf16[1,12,16,1536]{3,2,1,0:T(8,128)(2,1)} %param.23) | copy-start | bytes 1769476
  73.2 14.3 %copy-start.92 = (f32[1536]{0:T(1024)S(1)}, f32[1536]{0:T(1024)}, u32[]{:S(2)}) copy-start(f32[1536]{0:T(1024)} %param.20) | copy-start | bytes 18436
  87.5 13.3 %copy-start.90 = (f32[1536]{0:T(1024)S(1)}, f32[1536]{0:T(1024)}, u32[]{:S(2)}) copy-start(f32[1536]{0:T(1024)} %param.22) | copy-start | bytes 18436
  109.0 15.0 %collective-permute-start.11 = (bf16[2,3,16,1536]{3,2,1,0:T(8,128)(2,1)S(1)}, bf16[2,3,16,1536]{3,2,1,0:T(8,128)(2,1)}, u32[]{:S(2)}, u32[]{:S(2)}) collective-permute-start(bf16[2,3,16,1536]{3,2,1,0:T(8,128)(2,1)S(1)} %dynamic-slice_bitcast_fusion.2), channel_id=1, source_target_pairs={{0,1},{1,0},{2,3},{3,2},{4,5},{5,4},{6,7},{7,6},{8,9},{9,8},{10,11... | collective-permute-start | bytes 884744 | tf_op jit(solution)/shard_map/ppermute | solution.py:68
  125.2 9.5 %collective-permute-start.12 = (f32[1,3,16,1536]{3,2,1,0:T(8,128)S(1)}, f32[1,3,16,1536]{3,2,1,0:T(8,128)S(1)}, u32[]{:S(2)}, u32[]{:S(2)}) collective-permute-start(f32[1,3,16,1536]{3,2,1,0:T(8,128)S(1)} %constant_dynamic-slice_fusion.3), channel_id=1, source_target_pairs={{0,2},{1,3},{2,0},{3,1},{4,6},{5,7},{6,4},{7,5},{8,10},{9,11},{10,... | collective-permute-start | bytes 884744 | tf_op jit(solution)/shard_map/ppermute | solution.py:68
  129.3 15.9 %collective-permute-start.18 = (bf16[192,1536]{1,0:T(8,128)(2,1)}, bf16[192,1536]{1,0:T(8,128)(2,1)}, u32[]{:S(2)}, u32[]{:S(2)}) collective-permute-start(bf16[192,1536]{1,0:T(8,128)(2,1)} %get-tuple-element.132), channel_id=1, source_target_pairs={{0,8},{8,16},{16,24},{24,28},{28,20},{20,12},{12,4},{4,0},{1,9},{9... | collective-permute-start | bytes 1769480 | tf_op jit(solution)/shard_map/ppermute | solution.py:144
  131.1 59.7 %collective-permute-start.15 = (bf16[192,1536]{1,0:T(8,128)(2,1)S(1)}, bf16[192,1536]{1,0:T(8,128)(2,1)S(1)}, u32[]{:S(2)}, u32[]{:S(2)}) collective-permute-start(bf16[192,1536]{1,0:T(8,128)(2,1)S(1)} %get-tuple-element.131), channel_id=1, source_target_pairs={{0,4},{8,0},{16,8},{24,16},{28,24},{20,28},{12,20},{4,12},{1,5},{9... | collective-permute-start | bytes 1769480 | tf_op jit(solution)/shard_map/ppermute | solution.py:146
  136.6 12.2 %collective-permute-start.13 = (bf16[3,16,1536]{2,1,0:T(8,128)(2,1)S(1)}, bf16[3,16,1536]{2,1,0:T(8,128)(2,1)S(1)}, u32[]{:S(2)}, u32[]{:S(2)}) collective-permute-start(bf16[3,16,1536]{2,1,0:T(8,128)(2,1)S(1)} %get-tuple-element.120), channel_id=1, source_target_pairs={{0,1},{1,2},{2,3},{4,5},{5,6},{6,7},{8,9},{9,10},{10,11},{12,13},{... | collective-permute-start | bytes 442376 | tf_op jit(solution)/shard_map/ppermute | solution.py:15
  138.3 10.4 %collective-permute-start.14 = (bf16[3,16,1536]{2,1,0:T(8,128)(2,1)S(1)}, bf16[3,16,1536]{2,1,0:T(8,128)(2,1)}, u32[]{:S(2)}, u32[]{:S(2)}) collective-permute-start(bf16[3,16,1536]{2,1,0:T(8,128)(2,1)S(1)} %get-tuple-element.120), channel_id=1, source_target_pairs={{1,0},{2,1},{3,2},{5,4},{6,5},{7,6},{9,8},{10,9},{11,10},{13,12},{... | collective-permute-start | bytes 442376 | tf_op jit(solution)/shard_map/ppermute | solution.py:18
  142.0 7.9 %collective-permute-start.22 = (f32[2,18816]{1,0:T(2,128)S(1)}, f32[2,18816]{1,0:T(2,128)S(1)}, u32[]{:S(2)}, u32[]{:S(2)}) collective-permute-start(f32[2,18816]{1,0:T(2,128)S(1)} %bitcast.120), channel_id=1, source_target_pairs={{0,1},{1,0},{2,3},{3,2},{4,5},{5,4},{6,7},{7,6},{8,9},{9,8},{10,11... | collective-permute-start | bytes 451592 | tf_op jit(solution)/shard_map/ppermute | solution.py:68
  147.0 43.8 %collective-permute-start.19 = (bf16[192,1536]{1,0:T(8,128)(2,1)S(1)}, bf16[192,1536]{1,0:T(8,128)(2,1)S(1)}, u32[]{:S(2)}, u32[]{:S(2)}) collective-permute-start(bf16[192,1536]{1,0:T(8,128)(2,1)S(1)} %fusion.13), channel_id=1, source_target_pairs={{0,8},{8,16},{16,24},{24,28},{28,20},{20,12},{12,4},{4,0},{1,9},{9... | collective-permute-start | bytes 1769480 | tf_op jit(solution)/shard_map/ppermute | solution.py:144
  150.1 5.3 %collective-permute-start.23 = (f32[1,18816]{1,0:T(1,128)S(1)}, f32[1,18816]{1,0:T(1,128)S(1)}, u32[]{:S(2)}, u32[]{:S(2)}) collective-permute-start(f32[1,18816]{1,0:T(1,128)S(1)} %constant_dynamic-slice_fusion), channel_id=1, source_target_pairs={{0,2},{1,3},{2,0},{3,1},{4,6},{5,7},{6,4},{7,5},{8,10},{9,11},{10,... | collective-permute-start | bytes 225800 | tf_op jit(solution)/shard_map/ppermute | solution.py:68
  190.7 3.7 %collective-permute-start.24 = (f32[1,18816]{1,0:T(1,128)S(1)}, f32[1,18816]{1,0:T(1,128)S(1)}, u32[]{:S(2)}, u32[]{:S(2)}) collective-permute-start(f32[1,18816]{1,0:T(1,128)S(1)} %broadcast_in_dim.58), channel_id=1, source_target_pairs={{0,1},{1,0},{2,3},{3,2},{4,5},{5,4},{6,7},{7,6},{8,9},{9,8},{10,11... | collective-permute-start | bytes 225800 | tf_op jit(solution)/shard_map/ppermute | solution.py:169
  192.4 15.8 %collective-permute-start.16 = (bf16[192,1536]{1,0:T(8,128)(2,1)S(1)}, bf16[192,1536]{1,0:T(8,128)(2,1)S(1)}, u32[]{:S(2)}, u32[]{:S(2)}) collective-permute-start(bf16[192,1536]{1,0:T(8,128)(2,1)S(1)} %get-tuple-element.129), channel_id=1, source_target_pairs={{0,4},{8,0},{16,8},{24,16},{28,24},{20,28},{12,20},{4,12},{1,5},{9... | collective-permute-start | bytes 1769480 | tf_op jit(solution)/shard_map/ppermute | solution.py:146
  192.7 15.5 %collective-permute-start.20 = (bf16[192,1536]{1,0:T(8,128)(2,1)S(1)}, bf16[192,1536]{1,0:T(8,128)(2,1)S(1)}, u32[]{:S(2)}, u32[]{:S(2)}) collective-permute-start(bf16[192,1536]{1,0:T(8,128)(2,1)S(1)} %get-tuple-element.130), channel_id=1, source_target_pairs={{0,8},{8,16},{16,24},{24,28},{28,20},{20,12},{12,4},{4,0},{1,9},{9... | collective-permute-start | bytes 1769480 | tf_op jit(solution)/shard_map/ppermute | solution.py:144
  194.7 17.1 %collective-permute-start.25 = (f32[2,18816]{1,0:T(2,128)S(1)}, f32[2,18816]{1,0:T(2,128)S(1)}, u32[]{:S(2)}, u32[]{:S(2)}) collective-permute-start(f32[2,18816]{1,0:T(2,128)S(1)} %maximum_select_fusion.3), channel_id=1, source_target_pairs={{0,2},{1,3},{2,0},{3,1},{4,6},{5,7},{6,4},{7,5},{8,10},{9,11},{10,... | collective-permute-start | bytes 451592 | tf_op jit(solution)/shard_map/ppermute | solution.py:169
  209.7 14.9 %collective-permute-start.17 = (bf16[192,1536]{1,0:T(8,128)(2,1)S(1)}, bf16[192,1536]{1,0:T(8,128)(2,1)S(1)}, u32[]{:S(2)}, u32[]{:S(2)}) collective-permute-start(bf16[192,1536]{1,0:T(8,128)(2,1)S(1)} %get-tuple-element.127), channel_id=1, source_target_pairs={{0,4},{8,0},{16,8},{24,16},{28,24},{20,28},{12,20},{4,12},{1,5},{9... | collective-permute-start | bytes 1769480 | tf_op jit(solution)/shard_map/ppermute | solution.py:146
  210.0 15.2 %collective-permute-start.21 = (bf16[192,1536]{1,0:T(8,128)(2,1)S(1)}, bf16[192,1536]{1,0:T(8,128)(2,1)S(1)}, u32[]{:S(2)}, u32[]{:S(2)}) collective-permute-start(bf16[192,1536]{1,0:T(8,128)(2,1)S(1)} %get-tuple-element.128), channel_id=1, source_target_pairs={{0,8},{8,16},{16,24},{24,28},{28,20},{20,12},{12,4},{4,0},{1,9},{9... | collective-permute-start | bytes 1769480 | tf_op jit(solution)/shard_map/ppermute | solution.py:144
  (55 other events, 268.2 us)
